TPU v7x, 32 devices: a whole 2x2x4 slice. The times are simulated.
32 devices in a mesh: groups: 2 (over y), ctx: 4 (over z), mp: 4 (over x, core).
Axes of the slice: x: 2, y: 2, z: 4, core: 2. Of those that a mesh axis runs over, the one named last changes fastest.
Arguments:
- features: bfloat16 [4, 512, 1536], P('groups', 'ctx'), parts along dimension 0, may hold values from -6 to 6
- frame_counts: int32 [4], P('groups'), parts along dimension 0, may hold values from 1 to 512, 768 in all
- attn_gain: float32 [1536], replicated, may hold values from 0.25 to 1.75
- w_qkv: bfloat16 [3, 1536, 1024], P(None, None, 'mp'), may hold values from -2 to 2
- w_out: bfloat16 [1024, 1536], P('mp'), may hold values from -0.375 to 0.375
- conv_gain: float32 [1536], replicated, may hold values from 0.25 to 1.75
- w_glu: bfloat16 [2, 1536, 1536], P(None, None, 'mp'), may hold values from -0.15625 to 0.15625
- kernel: float32 [31, 1536], P(None, 'mp'), may hold values from -2 to 2
- bn_scale: float32 [1536], P('mp'), may hold values from 0.5 to 2
- bn_shift: float32 [1536], P('mp'), may hold values from -2.5 to 2.5
- w_pw: bfloat16 [1536, 1536], P('mp'), may hold values from -0.15625 to 0.15625
- clip_level: int32 [1536], replicated, may hold values from 6 to 39
Outputs:
- encoded: bfloat16 [4, 512, 1536], P('groups', ('ctx', 'mp')), parts along dimension 0
There are 2 independent parts, one for each index of `groups`. A program takes and returns all parts, laid end to end along the dimension named above; an argument that names none is the same for every part. Nothing has to cross between parts.
Inputs may be any that keep to these rules, and one draw needn't show every extreme that they name: frame_counts[s] frames of recording s fill slots 0 to frame_counts[s] - 1, later slots are padding; some recording fills all 512 slots.
All inputs are finite; a program needn't handle non-finite values.
Results may differ from a plain program's by a relative error of at most 0.023.
Values may be sent and summed in bfloat16 or wider, within the bound.
No kernel may reach another device: no remote copies, remote signals or barrier semaphores. Data moves between devices by JAX's collectives and lax.ppermute only.
A program may use at most 128 MiB of HBM per device.

v0:
```python
import jax
import jax.numpy as jnp
from jax import lax
from jax.sharding import PartitionSpec as P

HEAD_DIM = 64
epsilon = 1e-05
masked_score = -1e30


def with_halo(x, sides, width):
    for axis, dim in sides:
        devices, length = (lax.axis_size(axis), x.shape[dim])
        up = [(i, (i + 1) % devices) for i in range(devices - 1)]
        down = [(j, i) for i, j in up]
        last = lax.slice_in_dim(x, length - width, length, axis=dim)
        initial = lax.slice_in_dim(x, 0, width, axis=dim)
        before = lax.ppermute(last, axis, up)
        after = lax.ppermute(initial, axis, down)
        x = jnp.concatenate([before, x, after], axis=dim)
    return x


def layer_norm(values, gain):
    centre = jnp.mean(values, axis=-1, keepdims=True)
    centred = values - centre
    variance = jnp.mean(centred * centred, axis=-1, keepdims=True)
    return centred * lax.rsqrt(variance + epsilon) * gain


def gated_units(normed, w_glu):
    halves = jnp.einsum("std,gdc->gstc", normed, w_glu, preferred_element_type=jnp.float32)
    return (halves[0] * jax.nn.sigmoid(halves[1])).astype(jnp.bfloat16)


def shards(
    features,
    frame_counts,
    attn_gain,
    w_qkv,
    w_out,
    conv_gain,
    w_glu,
    kernel,
    bn_scale,
    bn_shift,
    w_pw,
    clip_level,
):
    records, frames_here, model_width = features.shape
    head_count = w_qkv.shape[2] // HEAD_DIM
    ctx_rank = lax.axis_index("ctx")
    score_scale = HEAD_DIM ** (-0.5)
    first_frame = ctx_rank * frames_here
    normed = layer_norm(features.astype(jnp.float32), attn_gain).astype(jnp.bfloat16)
    projected = jnp.einsum(
        "std,idc->istc", normed, w_qkv, preferred_element_type=jnp.float32
    ).astype(jnp.bfloat16)
    queries, key_rows, value_rows = (projected[0], projected[1], projected[2])
    query_heads = queries.reshape(records, frames_here, head_count, HEAD_DIM)
    start_max = jnp.full((records, head_count, frames_here), masked_score, jnp.float32)
    pieces = (
        lax.all_gather(key_rows, "ctx", axis=1, tiled=True),
        lax.all_gather(value_rows, "ctx", axis=1, tiled=True),
    )
    key_count = pieces[0].shape[1]
    key_heads = pieces[0].reshape(records, key_count, head_count, HEAD_DIM)
    value_heads = pieces[1].reshape(records, key_count, head_count, HEAD_DIM)
    scores = (
        jnp.einsum("sqhe,skhe->shqk", query_heads, key_heads, preferred_element_type=jnp.float32)
        * score_scale
    )
    positions = jnp.arange(key_count, dtype=jnp.int32)
    is_live = positions[None, :] < frame_counts[:, None]
    scores = jnp.where(is_live[:, None, None, :], scores, masked_score)
    new_max = jnp.maximum(start_max, jnp.max(scores, axis=-1))
    weights = jnp.exp(scores - new_max[..., None])
    new_sum = jnp.sum(weights, axis=-1)
    contrib = jnp.einsum(
        "shqk,skhe->shqe",
        weights.astype(jnp.bfloat16),
        value_heads,
        preferred_element_type=jnp.float32,
    )
    attended = (contrib / new_sum[..., None]).astype(jnp.bfloat16)
    attended = attended.transpose(0, 2, 1, 3).reshape(records, frames_here, head_count * HEAD_DIM)
    attn_part = jnp.einsum("stc,cd->std", attended, w_out, preferred_element_type=jnp.float32)
    mp_count = lax.axis_size("mp")
    mp_rank = lax.axis_index("mp")
    rows_mine = frames_here // mp_count
    row_start = mp_rank * rows_mine
    attn_sum = lax.psum(attn_part.astype(jnp.bfloat16), "mp").astype(jnp.float32)
    residual = features.astype(jnp.float32) + attn_sum
    gated_rows = gated_units(layer_norm(residual, conv_gain).astype(jnp.bfloat16), w_glu)
    residual_mine = lax.dynamic_slice_in_dim(residual, row_start, rows_mine, 1)
    frame_ids = first_frame + jnp.arange(frames_here, dtype=jnp.int32)
    frame_live = frame_ids[None, :] < frame_counts[:, None]
    gated_rows = jnp.where(frame_live[..., None], gated_rows, jnp.zeros((), jnp.bfloat16))
    rim_width = kernel.shape[0] // 2
    padded = with_halo(gated_rows, (("ctx", 1),), rim_width)
    depthwise = jnp.zeros(gated_rows.shape, jnp.float32)
    for tap_index in range(kernel.shape[0]):
        depthwise = (
            depthwise
            + padded[:, tap_index : tap_index + frames_here, :].astype(jnp.float32)
            * kernel[tap_index]
        )
    activated = jax.nn.silu(depthwise * bn_scale + bn_shift).astype(jnp.bfloat16)
    conv_part = jnp.einsum("stc,cd->std", activated, w_pw, preferred_element_type=jnp.float32)
    conv_rows = lax.psum_scatter(
        conv_part.astype(jnp.bfloat16), "mp", scatter_dimension=1, tiled=True
    ).astype(jnp.float32)
    combined = residual_mine + conv_rows
    clip_bound = clip_level.astype(jnp.float32) / 16.0
    clipped = jnp.clip(combined, -clip_bound, clip_bound)
    mine_ids = first_frame + row_start + jnp.arange(rows_mine, dtype=jnp.int32)
    mine_live = mine_ids[None, :] < frame_counts[:, None]
    return jnp.where(mine_live[..., None], clipped, 0.0).astype(jnp.bfloat16)


def solution(mesh):
    return jax.shard_map(
        shards,
        mesh=mesh,
        in_specs=(
            P("groups", "ctx", None),
            P("groups"),
            P(),
            P(None, None, "mp"),
            P("mp", None),
            P(),
            P(None, None, "mp"),
            P(None, "mp"),
            P("mp"),
            P("mp"),
            P("mp", None),
            P(),
        ),
        out_specs=P("groups", ("ctx", "mp"), None),
        check_vma=False,
    )
```

profile of v0, /device:TPU:0, one launch (start us, length us, event | category | flops | bytes accessed | tf_op | source)
XLA Modules:
  0.0 141.7 jit_solution(3153262464073058169)
XLA Ops:
  6.5 1.5 %convert_reduce_fusion = f32[2,128]{1,0:T(2,128)S(1)} fusion(bf16[2,128,1536]{2,1,0:T(8,128)(2,1)} %param.12), kind=kLoop, calls=%fused_computation.4 | loop fusion | flops 786176 | bytes 787456 | tf_op jit(solution)/shard_map/reduce_sum | solution.py:25
  8.0 1.5 %fusion.9 = f32[2,128]{1,0:T(2,128)S(1)} fusion(bf16[2,128,1536]{2,1,0:T(8,128)(2,1)} %param.12, f32[2,128]{1,0:T(2,128)S(1)} %broadcast_multiply_fusion.1), kind=kLoop, calls=%fused_computation.16 | loop fusion | flops 1572608 | bytes 788480 | tf_op jit(solution)/shard_map/reduce_sum | solution.py:27
  9.5 0.8 fusion.18
  10.5 18.0 %all-gather = bf16[1,2,512,256]{3,2,0,1:T(8,128)(2,1)} all-gather(bf16[1,2,128,256]{3,2,0,1:T(8,128)(2,1)S(1)} %get-tuple-element.38), channel_id=2, replica_groups=mesh['groups'=2,'ctx'=4,'mp'=4] {'ctx'}, dimensions={2}, use_global_device_ids=true | all-gather | bytes 655360 | tf_op jit(solution)/shard_map/all_gather | solution.py:63
  28.5 2.0 %copy.18 = bf16[1,2,512,256]{2,3,1,0:T(8,128)(2,1)} copy(bf16[1,2,512,256]{3,2,0,1:T(8,128)(2,1)} %all-gather) | data formatting | bytes 1048576 | tf_op jit(solution)/shard_map/all_gather | solution.py:63
  30.5 0.1 copy.17
  30.6 0.1 iota_compare_fusion
  30.7 2.9 %fusion.6 = (f32[2,4,128]{2,1,0:T(4,128)S(1)}, f32[2,4,128,512]{3,2,1,0:T(8,128)}) fusion(pred[2,512]{1,0:T(4,128)(4,1)S(1)} %iota_compare_fusion, bf16[2,128,4,64]{1,3,2,0:T(8,128)(2,1)S(1)} %bitcast.50, bf16[2,512,4,64]{1,3,2,0:T(8,128)(2,1)} %bitcast.49), kind=kOutput, calls=%fused_computation.13 | convolution fusion | flops 68680704 | bytes 2757632 | tf_op jit(solution)/shard_map/sqhe,skhe->shqk/dot_general | solution.py:70
  33.6 17.0 %all-gather.1 = bf16[1,2,512,256]{3,2,0,1:T(8,128)(2,1)} all-gather(bf16[1,2,128,256]{3,2,0,1:T(8,128)(2,1)S(1)} %get-tuple-element.39), channel_id=3, replica_groups=mesh['groups'=2,'ctx'=4,'mp'=4] {'ctx'}, dimensions={2}, use_global_device_ids=true | all-gather | bytes 655360 | tf_op jit(solution)/shard_map/all_gather | solution.py:64
  50.6 2.1 %copy.19 = bf16[1,2,512,256]{2,3,1,0:T(8,128)(2,1)} copy(bf16[1,2,512,256]{3,2,0,1:T(8,128)(2,1)} %all-gather.1) | data formatting | bytes 1048576 | tf_op jit(solution)/shard_map/all_gather | solution.py:64
  52.6 2.3 %fusion.7 = f32[2,4,128]{2,1,0:T(4,128)S(1)} fusion(f32[2,4,128,512]{3,2,1,0:T(8,128)} %get-tuple-element.46, f32[2,4,128]{2,1,0:T(4,128)S(1)} %broadcast_maximum_fusion, pred[2,512]{1,0:T(4,128)(4,1)S(1)} %iota_compare_fusion), kind=kLoop, calls=%fused_computation.14 | loop fusion | flops 2096128 | bytes 2106368 | tf_op jit(solution)/shard_map/reduce_sum | solution.py:78
  55.0 1.8 %fusion.23 = bf16[2,128,4,64]{1,3,2,0:T(8,128)(2,1)S(1)} fusion(bf16[2,512,4,64]{1,3,2,0:T(8,128)(2,1)} %bitcast.51, f32[2,4,128,512]{3,2,1,0:T(8,128)S(1)} %copy-done.2, f32[2,4,128]{2,1,0:T(4,128)S(1)} %broadcast_maximum_fusion, pred[2,512]{1,0:T(4,128)(4,1)S(1)} %iota_compare_fusion, f32[2,128,4]{1,2,0:T(4,128)S(1)} %bitcast.53), kind=kOutput, calls=%fused_computation.55 | convolution fusion | flops 69337088 | bytes 2761728 | tf_op jit(solution)/shard_map/shqk,skhe->shqe/dot_general | solution.py:79
  56.8 1.3 convolution_convert_fusion
  58.1 0.0 all-reduce.2.cloned.1.call-update
  58.1 0.0 reduce-scatter.2.cloned.1.call-start
  58.2 0.1 slice_reduce_fusion.30
  58.3 0.1 broadcast_compare_fusion
  58.3 35.0 %all-reduce.2.cloned.1.call-done = bf16[2,128,1536]{2,1,0:T(8,128)(2,1)} async-done(((bf16[2,128,1536]{2,1,0:T(8,128)(2,1)}), bf16[2,128,1536]{2,1,0:T(8,128)(2,1)}) %all-reduce.2.cloned.1.call-update) | async-done | bytes 786448 | tf_op jit(solution)/shard_map/psum | solution.py:92
  93.3 2.6 %convert_add_fusion = (f32[2,128,1536]{2,1,0:T(8,128)}, f32[2,128]{1,0:T(2,128)S(1)}) fusion(bf16[2,128,1536]{2,1,0:T(8,128)(2,1)S(1)} %copy-done.1, bf16[2,128,1536]{2,1,0:T(8,128)(2,1)} %all-reduce.2.cloned.1.call-done), kind=kLoop, calls=%fused_computation.2 | loop fusion | flops 1572608 | bytes 3146752 | tf_op jit(solution)/shard_map/add | solution.py:93
  96.0 0.4 multiply_reduce_fusion
  96.4 0.3 copy-done.11
  96.7 1.0 fusion.12
  97.7 0.1 bitcast_select_fusion
  97.8 3.4 %collective-permute-start = (bf16[2,15,384]{2,1,0:T(8,128)(2,1)S(1)}, bf16[2,15,384]{2,1,0:T(8,128)(2,1)S(1)}, u32[]{:S(2)}, u32[]{:S(2)}) collective-permute-start(bf16[2,15,384]{2,1,0:T(8,128)(2,1)S(1)} %get-tuple-element.41), channel_id=1, source_target_pairs={{0,4},{4,8},{8,12},{1,5},{5,9},{9,13},{2,6},{6,10},{10,14},{3,7},{... | collective-permute-start | bytes 69128 | tf_op jit(solution)/shard_map/ppermute | solution.py:18
  101.2 1.3 collective-permute-start.1
  102.5 0.1 slice_reduce_fusion.29
  102.6 0.1 collective-permute-done
  102.7 4.2 %collective-permute-done.1 = bf16[2,15,384]{2,1,0:T(8,128)(2,1)S(1)} collective-permute-done((bf16[2,15,384]{2,1,0:T(8,128)(2,1)S(1)}, bf16[2,15,384]{2,1,0:T(8,128)(2,1)S(1)}, u32[]{:S(2)}, u32[]{:S(2)}) %collective-permute-start.1) | collective-permute-done | bytes 23072 | tf_op jit(solution)/shard_map/ppermute | solution.py:19
  107.0 3.5 %convolution_convert_fusion.1 = bf16[2,128,1536]{2,1,0:T(8,128)(2,1)} fusion(bf16[384,1536]{1,0:T(8,128)(2,1)S(1)} %copy-done.9, bf16[2,128,384]{2,1,0:T(8,128)(2,1)S(1)} %bitcast_select_fusion, bf16[2,15,384]{2,1,0:T(8,128)(2,1)S(1)} %collective-permute-done.1, bf16[2,15,384]{2,1,0:T(8,128)(2,1)S(1)} %collective-permute-done, f32[384]{0:T(512)S(1)} %copy-done.12, ...), kind=kOutput, calls=%fused_computation.1 | convolution fusion | flops 320962560 | bytes 2259456 | tf_op jit(solution)/shard_map/stc,cd->std/dot_general | solution.py:109
  110.5 0.1 broadcast_compare_fusion.1
  110.6 22.4 %reduce-scatter.2.cloned.1.call-done = bf16[2,32,1536]{2,1,0:T(8,128)(2,1)} async-done(((bf16[2,128,1536]{2,1,0:T(8,128)(2,1)}), bf16[2,32,1536]{2,1,0:T(8,128)(2,1)}) %reduce-scatter.2.cloned.1.call-update) | async-done | bytes 196624 | tf_op jit(solution)/shard_map/reduce_scatter | solution.py:110
  133.0 1.9 %select_convert_fusion = bf16[2,32,1536]{2,1,0:T(8,128)(2,1)} fusion(bf16[2,32,1536]{2,1,0:T(8,128)(2,1)} %reduce-scatter.2.cloned.1.call-done, f32[2,128,1536]{2,1,0:T(8,128)} %get-tuple-element.36, s32[]{:T(128)S(6)} %select_n.16, bf16[1536]{0:T(1024)(128)(2,1)S(1)} %get-tuple-element.44, bf16[1536]{0:T(1024)(128)(2,1)S(1)} %get-tuple-element.43, ...), kind=kLoop, calls=%fused_computation.74 | loop fusion | flops 786432 | bytes 792644 | tf_op jit(solution)/shard_map/convert_element_type | solution.py:118
  (39 shorter events, 0.2 us)
Async XLA Ops:
  6.5 3.0 %copy-start = (bf16[3,1536,256]{2,1,0:T(8,128)(2,1)S(1)}, bf16[3,1536,256]{2,1,0:T(8,128)(2,1)}, u32[]{:S(2)}) copy-start(bf16[3,1536,256]{2,1,0:T(8,128)(2,1)} %param.15) | copy-start | bytes 7077892
  6.5 3.0 %copy-start.1 = (bf16[2,128,1536]{2,1,0:T(8,128)(2,1)S(1)}, bf16[2,128,1536]{2,1,0:T(8,128)(2,1)}, u32[]{:S(2)}) copy-start(bf16[2,128,1536]{2,1,0:T(8,128)(2,1)} %param.12) | copy-start | bytes 2359300
  6.5 3.0 %copy-start.10 = (f32[1536]{0:T(1024)S(1)}, f32[1536]{0:T(1024)}, u32[]{:S(2)}) copy-start(f32[1536]{0:T(1024)} %param.14) | copy-start | bytes 18436
  6.5 86.8 %all-reduce.2.cloned.1.call-start = ((), (), s32[]{:S(2)}) async-start(), calls=%async_computation.1 | async-start | bytes 1572864 | tf_op jit(solution)/shard_map/psum | solution.py:92
  10.4 20.2 %copy-start.7 = (s32[2]{0:T(128)S(1)}, s32[2]{0:T(128)}, u32[]{:S(2)}) copy-start(s32[2]{0:T(128)} %param.13) | copy-start | bytes 28
  52.6 2.3 %copy-start.2 = (f32[2,4,128,512]{3,2,1,0:T(8,128)S(1)}, f32[2,4,128,512]{3,2,1,0:T(8,128)}, u32[]{:S(2)}) copy-start(f32[2,4,128,512]{3,2,1,0:T(8,128)} %get-tuple-element.46) | copy-start | bytes 6291460
  55.0 1.8 %copy-start.4 = (bf16[256,1536]{1,0:T(8,128)(2,1)S(1)}, bf16[256,1536]{1,0:T(8,128)(2,1)}, u32[]{:S(2)}) copy-start(bf16[256,1536]{1,0:T(8,128)(2,1)} %param.16) | copy-start | bytes 2359300
  56.8 1.4 copy-start.5
  58.1 74.9 %reduce-scatter.2.cloned.1.call-start = ((), (), s32[]{:S(2)}) async-start(), calls=%async_computation.2 | async-start | bytes 983040 | tf_op jit(solution)/shard_map/reduce_scatter | solution.py:110
  93.3 2.7 %copy-start.3 = (bf16[2,128,1536]{2,1,0:T(8,128)(2,1)S(1)}, bf16[2,128,1536]{2,1,0:T(8,128)(2,1)}, u32[]{:S(2)}) copy-start(bf16[2,128,1536]{2,1,0:T(8,128)(2,1)} %all-reduce.2.cloned.1.call-done) | copy-start | bytes 2359300
  93.3 3.1 %copy-start.8 = (bf16[2,1536,384]{2,1,0:T(8,128)(2,1)S(1)}, bf16[2,1536,384]{2,1,0:T(8,128)(2,1)}, u32[]{:S(2)}) copy-start(bf16[2,1536,384]{2,1,0:T(8,128)(2,1)} %param.18) | copy-start | bytes 7077892
  96.0 0.7 copy-start.11
  96.7 10.2 %copy-start.9 = (bf16[384,1536]{1,0:T(8,128)(2,1)S(1)}, bf16[384,1536]{1,0:T(8,128)(2,1)}, u32[]{:S(2)}) copy-start(bf16[384,1536]{1,0:T(8,128)(2,1)} %param.22) | copy-start | bytes 3538948
  96.7 10.2 %copy-start.12 = (f32[384]{0:T(512)S(1)}, f32[384]{0:T(512)}, u32[]{:S(2)}) copy-start(f32[384]{0:T(512)} %param.21) | copy-start | bytes 4612
  96.7 10.2 %copy-start.13 = (f32[384]{0:T(512)S(1)}, f32[384]{0:T(512)}, u32[]{:S(2)}) copy-start(f32[384]{0:T(512)} %param.20) | copy-start | bytes 4612
  97.8 4.9 %collective-permute-start = (bf16[2,15,384]{2,1,0:T(8,128)(2,1)S(1)}, bf16[2,15,384]{2,1,0:T(8,128)(2,1)S(1)}, u32[]{:S(2)}, u32[]{:S(2)}) collective-permute-start(bf16[2,15,384]{2,1,0:T(8,128)(2,1)S(1)} %get-tuple-element.41), channel_id=1, source_target_pairs={{0,4},{4,8},{8,12},{1,5},{5,9},{9,13},{2,6},{6,10},{10,14},{3,7},{... | collective-permute-start | bytes 69128 | tf_op jit(solution)/shard_map/ppermute | solution.py:18
  101.2 5.7 %collective-permute-start.1 = (bf16[2,15,384]{2,1,0:T(8,128)(2,1)S(1)}, bf16[2,15,384]{2,1,0:T(8,128)(2,1)S(1)}, u32[]{:S(2)}, u32[]{:S(2)}) collective-permute-start(bf16[2,15,384]{2,1,0:T(8,128)(2,1)S(1)} %get-tuple-element.42), channel_id=1, source_target_pairs={{4,0},{8,4},{12,8},{5,1},{9,5},{13,9},{6,2},{10,6},{14,10},{7,3},{... | collective-permute-start | bytes 69128 | tf_op jit(solution)/shard_map/ppermute | solution.py:19
  106.9 3.7 %copy-start.6 = (s32[1536]{0:T(1024)S(1)}, s32[1536]{0:T(1024)}, u32[]{:S(2)}) copy-start(s32[1536]{0:T(1024)} %param.23) | copy-start | bytes 18436
Sparse Core Ops, SparseCore 0:
  58.2 35.0 all-reduce.1
  110.6 22.3 reduce-scatter.1
where the time goes:
time: 142 us
  waiting for transfers between devices  61.8 us (44%)
  blocking collectives  35 us (25%)
  between operations  13.6 us (10%)
  matrix products  11.3 us (8%)
  other arithmetic  10.6 us (7%)
  local copies, waits for them, and re-layouts  4.75 us (3%)
  starting transfers between devices  4.72 us (3%)
    psum x1, waiting for transfers between devices, shards(): lax.psum(attn_part.astype(jnp.bfloat16), 'mp').astype(jnp.float32)  35 us
    reduce_scatter x1, waiting for transfers between devices, shards(): lax.psum_scatter(conv_part.astype(jnp.bfloat16), 'mp', scatter_dimension=...  22.4 us
    all_gather x1, blocking collectives, shards(): lax.all_gather(key_rows, 'ctx', axis=1, tiled=True)  18 us
    all_gather x1, blocking collectives, shards(): lax.all_gather(value_rows, 'ctx', axis=1, tiled=True)  17 us
    ppermute x1, waiting for transfers between devices, with_halo(): after = lax.ppermute(initial, axis, down)  4.22 us
    dot_general x1, matrix products, shards(): jnp.einsum('stc,cd->std', activated, w_pw, preferred_element_type=jnp.flo...  3.55 us
    ppermute x1, starting transfers between devices, with_halo(): before = lax.ppermute(last, axis, up)  3.39 us
    dot_general x1, matrix products, shards(): jnp.einsum('sqhe,skhe->shqk', query_heads, key_heads, preferred_element_t...  2.88 us
  transfers between devices with their start and end apart: 4, of which 4 were waited for; matrix products, arithmetic and copies ran while one was open for 0% of the time, Pallas kernels for 0%

commit v1 on v0

--- a/solution.py
+++ b/solution.py
@@ -1,3 +1,4 @@
+import functools
 import jax
 import jax.numpy as jnp
 from jax import lax
@@ -6,6 +7,32 @@
 HEAD_DIM = 64
 epsilon = 1e-05
 masked_score = -1e30
+
+
+def _fix_arrays(x_part, net_axis):
+    z, piece_next, spare = (
+        jax.lax.psum(1, net_axis),
+        jax.lax.axis_index(net_axis),
+        x_part.shape[1],
+    )
+    views = tuple(((i0, (i0 + 1) % z) for i0 in range(z)))
+    vals = tuple(((i0, (i0 - 1) % z) for i0 in range(z)))
+    new = jnp.zeros((*x_part.shape[:1], z * spare, *x_part.shape[2:]), x_part.dtype)
+    new = lax.dynamic_update_slice_in_dim(new, x_part, piece_next * spare, axis=1)
+    vec_out = z // 2
+    odd = value_now = x_part
+    for j0 in tuple(range(1, vec_out + 1)):
+        odd = jax.lax.ppermute(odd, net_axis, views)
+        new = lax.dynamic_update_slice_in_dim(new, odd, (piece_next - j0) % z * spare, axis=1)
+        if j0 < z - vec_out:
+            value_now = jax.lax.ppermute(value_now, net_axis, vals)
+            new = lax.dynamic_update_slice_in_dim(
+                new, value_now, (piece_next + j0) % z * spare, axis=1
+            )
+    return new
+
+
+pair_members_all = functools.partial(_fix_arrays, net_axis="ctx")
 
 
 def with_halo(x, sides, width):
@@ -59,10 +86,7 @@
     queries, key_rows, value_rows = (projected[0], projected[1], projected[2])
     query_heads = queries.reshape(records, frames_here, head_count, HEAD_DIM)
     start_max = jnp.full((records, head_count, frames_here), masked_score, jnp.float32)
-    pieces = (
-        lax.all_gather(key_rows, "ctx", axis=1, tiled=True),
-        lax.all_gather(value_rows, "ctx", axis=1, tiled=True),
-    )
+    pieces = (lax.all_gather(key_rows, "ctx", axis=1, tiled=True), pair_members_all(value_rows))
     key_count = pieces[0].shape[1]
     key_heads = pieces[0].reshape(records, key_count, head_count, HEAD_DIM)
     value_heads = pieces[1].reshape(records, key_count, head_count, HEAD_DIM)

time: 142 us -> 136 us (0.958)
  blocking collectives: 35 us -> 17.8 us
  starting transfers between devices: 4.72 us -> 10.2 us
  local copies, waits for them, and re-layouts: 4.75 us -> 9.88 us
  waiting for transfers between devices: 61.8 us -> 64.2 us
  other arithmetic: 10.6 us -> 8.87 us
    all_gather x1 -> x0, blocking collectives: 17 us -> none  [shards(): lax.all_gather(value_rows, 'ctx', axis=1, tiled=True)]
    ppermute x0 -> x3, starting transfers between devices: none -> 5.49 us  [the longest x2 3.39 us: _fix_arrays(): odd = jax.lax.ppermute(odd, net_axis, views)]
    ppermute x0 -> x3, waiting for transfers between devices: none -> 4.32 us  [the longest x2 4.31 us: _fix_arrays(): odd = jax.lax.ppermute(odd, net_axis, views)]
    dynamic_update_slice x0 -> x4, local copies, waits for them, and re-layouts: none -> 2.71 us  [the longest x2 1.37 us: _fix_arrays(): lax.dynamic_update_slice_in_dim(new, odd, (piece_next - j0) % z * spare,...]
    ppermute x0 -> x3, local copies, waits for them, and re-layouts: none -> 2.16 us  [the longest x2 1.14 us: _fix_arrays(): odd = jax.lax.ppermute(odd, net_axis, views)]
    all_gather x1 -> x0, local copies, waits for them, and re-layouts: 2.05 us -> none  [shards(): lax.all_gather(value_rows, 'ctx', axis=1, tiled=True)]
    psum x1, waiting for transfers between devices: 35 us -> 33 us  [shards(): lax.psum(attn_part.astype(jnp.bfloat16), 'mp').astype(jnp.float32)]
    reduce_sum x1, other arithmetic: 2.3 us -> 0.61 us  [shards(): new_sum = jnp.sum(weights, axis=-1)]
  transfers between devices with their start and end apart: 4 -> 7, of which waited for: 4 -> 5; matrix products, arithmetic and copies ran while one was open for 0% -> 7% of each run, Pallas kernels for 0% -> 0%
where the time goes in v1:
time: 136 us; the launch traced here: 135 us
  waiting for transfers between devices  64.2 us (47%)
  blocking collectives  17.8 us (13%)
  between operations  13.7 us (10%)
  matrix products  10.6 us (8%)
  starting transfers between devices  10.2 us (7%)
  local copies, waits for them, and re-layouts  9.88 us (7%)
  other arithmetic  8.87 us (7%)
    psum x1, waiting for transfers between devices, shards(): lax.psum(attn_part.astype(jnp.bfloat16), 'mp').astype(jnp.float32)  33 us
    reduce_scatter x1, waiting for transfers between devices, shards(): lax.psum_scatter(conv_part.astype(jnp.bfloat16), 'mp', scatter_dimension=...  22.5 us
    all_gather x1, blocking collectives, shards(): lax.all_gather(key_rows, 'ctx', axis=1, tiled=True)  17.8 us
    ppermute x2, waiting for transfers between devices, _fix_arrays(): odd = jax.lax.ppermute(odd, net_axis, views)  4.31 us
    ppermute x1, waiting for transfers between devices, with_halo(): after = lax.ppermute(initial, axis, down)  4.22 us
    dot_general x1, matrix products, shards(): jnp.einsum('stc,cd->std', activated, w_pw, preferred_element_type=jnp.flo...  3.52 us
    ppermute x2, starting transfers between devices, _fix_arrays(): odd = jax.lax.ppermute(odd, net_axis, views)  3.39 us
    ppermute x1, starting transfers between devices, with_halo(): before = lax.ppermute(last, axis, up)  3.39 us
  transfers between devices with their start and end apart: 7, of which 5 were waited for; matrix products, arithmetic and copies ran while one was open for 7% of the time, Pallas kernels for 0%

profile of v1, /device:TPU:0, one launch (start us, length us, event | category | flops | bytes accessed | tf_op | source)
XLA Modules:
  0.0 135.2 jit_solution(325660195085175890)
XLA Ops:
  6.5 1.5 %convert_reduce_fusion = f32[2,128]{1,0:T(2,128)S(1)} fusion(bf16[2,128,1536]{2,1,0:T(8,128)(2,1)} %param.12), kind=kLoop, calls=%fused_computation.4 | loop fusion | flops 786176 | bytes 787456 | tf_op jit(solution)/shard_map/reduce_sum | solution.py:52
  8.0 1.5 %fusion.9 = f32[2,128]{1,0:T(2,128)S(1)} fusion(bf16[2,128,1536]{2,1,0:T(8,128)(2,1)} %param.12, f32[2,128]{1,0:T(2,128)S(1)} %broadcast_multiply_fusion.1), kind=kLoop, calls=%fused_computation.16 | loop fusion | flops 1572608 | bytes 788480 | tf_op jit(solution)/shard_map/reduce_sum | solution.py:54
  9.5 0.8 fusion.18
  10.5 3.1 %collective-permute-start = (bf16[2,128,256]{2,1,0:T(8,128)(2,1)S(1)}, bf16[2,128,256]{2,1,0:T(8,128)(2,1)}, u32[]{:S(2)}, u32[]{:S(2)}) collective-permute-start(bf16[2,128,256]{2,1,0:T(8,128)(2,1)S(1)} %get-tuple-element.39), channel_id=1, source_target_pairs={{0,4},{4,8},{8,12},{12,0},{1,5},{5,9},{9,13},{13,1},{2,6},{6,10},{... | collective-permute-start | bytes 393224 | tf_op jit(solution)/shard_map/ppermute | solution.py:25
  13.5 2.1 %collective-permute-start.1 = (bf16[2,128,256]{2,1,0:T(8,128)(2,1)S(1)}, bf16[2,128,256]{2,1,0:T(8,128)(2,1)}, u32[]{:S(2)}, u32[]{:S(2)}) collective-permute-start(bf16[2,128,256]{2,1,0:T(8,128)(2,1)S(1)} %get-tuple-element.39), channel_id=1, source_target_pairs={{0,12},{4,0},{8,4},{12,8},{1,13},{5,1},{9,5},{13,9},{2,14},{6,2},{... | collective-permute-start | bytes 393224 | tf_op jit(solution)/shard_map/ppermute | solution.py:28
  15.6 17.8 %all-gather = bf16[1,2,512,256]{3,2,0,1:T(8,128)(2,1)} all-gather(bf16[1,2,128,256]{3,2,0,1:T(8,128)(2,1)S(1)} %get-tuple-element.38), channel_id=2, replica_groups=mesh['groups'=2,'ctx'=4,'mp'=4] {'ctx'}, dimensions={2}, use_global_device_ids=true | all-gather | bytes 655360 | tf_op jit(solution)/shard_map/all_gather | solution.py:89
  33.4 2.1 %copy.21 = bf16[1,2,512,256]{2,3,1,0:T(8,128)(2,1)} copy(bf16[1,2,512,256]{3,2,0,1:T(8,128)(2,1)} %all-gather) | data formatting | bytes 1048576 | tf_op jit(solution)/shard_map/all_gather | solution.py:89
  35.7 1.6 %fusion.6 = (f32[2,4,128]{2,1,0:T(4,128)S(1)}, f32[2,4,128,512]{3,2,1,0:T(8,128)S(1)}) fusion(pred[2,512]{1,0:T(4,128)(4,1)S(1)} %iota_compare_fusion, bf16[2,128,4,64]{1,3,2,0:T(8,128)(2,1)S(1)} %bitcast.52, bf16[2,512,4,64]{1,3,2,0:T(8,128)(2,1)} %bitcast.51), kind=kOutput, calls=%fused_computation.13 | convolution fusion | flops 68680704 | bytes 2757632 | tf_op jit(solution)/shard_map/sqhe,skhe->shqk/dot_general | solution.py:94
  37.3 1.3 copy-done.2
  38.6 0.6 fusion.7
  39.4 0.8 broadcast_in_dim.44
  40.2 0.7 constant_dynamic-update-slice_fusion.3
  40.9 1.0 copy.23
  41.9 0.3 collective-permute-start.2
  42.2 0.7 constant_dynamic-update-slice_fusion.2
  42.9 1.0 copy.24
  43.9 0.7 constant_dynamic-update-slice_fusion.1
  44.6 4.3 %collective-permute-done.2 = bf16[2,128,256]{2,1,0:T(8,128)(2,1)S(1)} collective-permute-done((bf16[2,128,256]{2,1,0:T(8,128)(2,1)}, bf16[2,128,256]{2,1,0:T(8,128)(2,1)S(1)}, u32[]{:S(2)}, u32[]{:S(2)}) %collective-permute-start.2) | collective-permute-done | bytes 131104 | tf_op jit(solution)/shard_map/ppermute | solution.py:25
  49.1 0.7 constant_dynamic-update-slice_fusion
  49.7 2.4 %fusion.23 = bf16[2,128,4,64]{1,3,2,0:T(8,128)(2,1)S(1)} fusion(bf16[2,512,4,64]{1,3,2,0:T(8,128)(2,1)} %bitcast.7, f32[2,4,128,512]{3,2,1,0:T(8,128)} %copy-done.2, f32[2,4,128]{2,1,0:T(4,128)S(1)} %broadcast_maximum_fusion, pred[2,512]{1,0:T(4,128)(4,1)S(1)} %iota_compare_fusion, f32[2,128,4]{1,2,0:T(4,128)S(1)} %bitcast.54), kind=kOutput, calls=%fused_computation.55 | convolution fusion | flops 69337088 | bytes 2761728 | tf_op jit(solution)/shard_map/shqk,skhe->shqe/dot_general | solution.py:103
  52.2 1.3 convolution_convert_fusion
  53.7 33.0 %all-reduce.2.cloned.1.call-done = bf16[2,128,1536]{2,1,0:T(8,128)(2,1)} async-done(((bf16[2,128,1536]{2,1,0:T(8,128)(2,1)}), bf16[2,128,1536]{2,1,0:T(8,128)(2,1)}) %all-reduce.2.cloned.1.call-update) | async-done | bytes 786448 | tf_op jit(solution)/shard_map/psum | solution.py:116
  86.8 2.6 %convert_add_fusion = (f32[2,128,1536]{2,1,0:T(8,128)}, f32[2,128]{1,0:T(2,128)S(1)}) fusion(bf16[2,128,1536]{2,1,0:T(8,128)(2,1)S(1)} %copy-done.1, bf16[2,128,1536]{2,1,0:T(8,128)(2,1)} %all-reduce.2.cloned.1.call-done), kind=kLoop, calls=%fused_computation.2 | loop fusion | flops 1572608 | bytes 3146752 | tf_op jit(solution)/shard_map/add | solution.py:117
  89.4 0.4 multiply_reduce_fusion
  89.8 0.3 copy-done.11
  90.1 1.0 fusion.12
  91.2 3.4 %collective-permute-start.3 = (bf16[2,15,384]{2,1,0:T(8,128)(2,1)S(1)}, bf16[2,15,384]{2,1,0:T(8,128)(2,1)S(1)}, u32[]{:S(2)}, u32[]{:S(2)}) collective-permute-start(bf16[2,15,384]{2,1,0:T(8,128)(2,1)S(1)} %get-tuple-element.41), channel_id=1, source_target_pairs={{0,4},{4,8},{8,12},{1,5},{5,9},{9,13},{2,6},{6,10},{10,14},{3,7},{... | collective-permute-start | bytes 69128 | tf_op jit(solution)/shard_map/ppermute | solution.py:45
  94.6 1.3 collective-permute-start.4
  96.1 4.2 %collective-permute-done.4 = bf16[2,15,384]{2,1,0:T(8,128)(2,1)S(1)} collective-permute-done((bf16[2,15,384]{2,1,0:T(8,128)(2,1)S(1)}, bf16[2,15,384]{2,1,0:T(8,128)(2,1)S(1)}, u32[]{:S(2)}, u32[]{:S(2)}) %collective-permute-start.4) | collective-permute-done | bytes 23072 | tf_op jit(solution)/shard_map/ppermute | solution.py:46
  100.4 3.5 %convolution_convert_fusion.1 = bf16[2,128,1536]{2,1,0:T(8,128)(2,1)} fusion(bf16[384,1536]{1,0:T(8,128)(2,1)S(1)} %copy-done.9, bf16[2,128,384]{2,1,0:T(8,128)(2,1)S(1)} %bitcast_select_fusion, bf16[2,15,384]{2,1,0:T(8,128)(2,1)S(1)} %collective-permute-done.4, bf16[2,15,384]{2,1,0:T(8,128)(2,1)S(1)} %collective-permute-done.3, f32[384]{0:T(512)S(1)} %copy-done.12, ...), kind=kOutput, calls=%fused_computation.1 | convolution fusion | flops 320962560 | bytes 2259456 | tf_op jit(solution)/shard_map/stc,cd->std/dot_general | solution.py:133
  104.0 22.5 %reduce-scatter.2.cloned.1.call-done = bf16[2,32,1536]{2,1,0:T(8,128)(2,1)} async-done(((bf16[2,128,1536]{2,1,0:T(8,128)(2,1)}), bf16[2,32,1536]{2,1,0:T(8,128)(2,1)}) %reduce-scatter.2.cloned.1.call-update) | async-done | bytes 196624 | tf_op jit(solution)/shard_map/reduce_scatter | solution.py:134
  126.5 1.9 %select_convert_fusion = bf16[2,32,1536]{2,1,0:T(8,128)(2,1)} fusion(bf16[2,32,1536]{2,1,0:T(8,128)(2,1)} %reduce-scatter.2.cloned.1.call-done, f32[2,128,1536]{2,1,0:T(8,128)} %get-tuple-element.36, s32[]{:T(128)S(6)} %select_n.50, bf16[1536]{0:T(1024)(128)(2,1)S(1)} %get-tuple-element.44, bf16[1536]{0:T(1024)(128)(2,1)S(1)} %get-tuple-element.43, ...), kind=kLoop, calls=%fused_computation.74 | loop fusion | flops 786432 | bytes 792644 | tf_op jit(solution)/shard_map/convert_element_type | solution.py:142
  (52 shorter events, 1.2 us)
Async XLA Ops:
  6.5 3.0 %copy-start = (bf16[3,1536,256]{2,1,0:T(8,128)(2,1)S(1)}, bf16[3,1536,256]{2,1,0:T(8,128)(2,1)}, u32[]{:S(2)}) copy-start(bf16[3,1536,256]{2,1,0:T(8,128)(2,1)} %param.15) | copy-start | bytes 7077892
  6.5 3.0 %copy-start.1 = (bf16[2,128,1536]{2,1,0:T(8,128)(2,1)S(1)}, bf16[2,128,1536]{2,1,0:T(8,128)(2,1)}, u32[]{:S(2)}) copy-start(bf16[2,128,1536]{2,1,0:T(8,128)(2,1)} %param.12) | copy-start | bytes 2359300
  6.5 3.0 %copy-start.10 = (f32[1536]{0:T(1024)S(1)}, f32[1536]{0:T(1024)}, u32[]{:S(2)}) copy-start(f32[1536]{0:T(1024)} %param.14) | copy-start | bytes 18436
  6.5 80.2 %all-reduce.2.cloned.1.call-start = ((), (), s32[]{:S(2)}) async-start(), calls=%async_computation.1 | async-start | bytes 1572864 | tf_op jit(solution)/shard_map/psum | solution.py:116
  10.4 25.2 %copy-start.7 = (s32[2]{0:T(128)S(1)}, s32[2]{0:T(128)}, u32[]{:S(2)}) copy-start(s32[2]{0:T(128)} %param.13) | copy-start | bytes 28
  10.5 30.4 %collective-permute-start = (bf16[2,128,256]{2,1,0:T(8,128)(2,1)S(1)}, bf16[2,128,256]{2,1,0:T(8,128)(2,1)}, u32[]{:S(2)}, u32[]{:S(2)}) collective-permute-start(bf16[2,128,256]{2,1,0:T(8,128)(2,1)S(1)} %get-tuple-element.39), channel_id=1, source_target_pairs={{0,4},{4,8},{8,12},{12,0},{1,5},{5,9},{9,13},{13,1},{2,6},{6,10},{... | collective-permute-start | bytes 393224 | tf_op jit(solution)/shard_map/ppermute | solution.py:25
  13.5 29.4 %collective-permute-start.1 = (bf16[2,128,256]{2,1,0:T(8,128)(2,1)S(1)}, bf16[2,128,256]{2,1,0:T(8,128)(2,1)}, u32[]{:S(2)}, u32[]{:S(2)}) collective-permute-start(bf16[2,128,256]{2,1,0:T(8,128)(2,1)S(1)} %get-tuple-element.39), channel_id=1, source_target_pairs={{0,12},{4,0},{8,4},{12,8},{1,13},{5,1},{9,5},{13,9},{2,14},{6,2},{... | collective-permute-start | bytes 393224 | tf_op jit(solution)/shard_map/ppermute | solution.py:28
  37.3 1.4 %copy-start.2 = (f32[2,4,128,512]{3,2,1,0:T(8,128)}, f32[2,4,128,512]{3,2,1,0:T(8,128)S(1)}, u32[]{:S(2)}) copy-start(f32[2,4,128,512]{3,2,1,0:T(8,128)S(1)} %get-tuple-element.46) | copy-start | bytes 6291460
  41.9 7.0 %collective-permute-start.2 = (bf16[2,128,256]{2,1,0:T(8,128)(2,1)}, bf16[2,128,256]{2,1,0:T(8,128)(2,1)S(1)}, u32[]{:S(2)}, u32[]{:S(2)}) collective-permute-start(bf16[2,128,256]{2,1,0:T(8,128)(2,1)} %collective-permute-done), channel_id=1, source_target_pairs={{0,4},{4,8},{8,12},{12,0},{1,5},{5,9},{9,13},{13,1},{2,6},{6,10},{... | collective-permute-start | bytes 393224 | tf_op jit(solution)/shard_map/ppermute | solution.py:25
  49.7 2.4 %copy-start.4 = (bf16[256,1536]{1,0:T(8,128)(2,1)S(1)}, bf16[256,1536]{1,0:T(8,128)(2,1)}, u32[]{:S(2)}) copy-start(bf16[256,1536]{1,0:T(8,128)(2,1)} %param.16) | copy-start | bytes 2359300
  52.2 1.4 %copy-start.5 = (f32[31,384]{1,0:T(8,128)S(1)}, f32[31,384]{1,0:T(8,128)}, u32[]{:S(2)}) copy-start(f32[31,384]{1,0:T(8,128)} %param.19) | copy-start | bytes 142852
  53.5 73.0 %reduce-scatter.2.cloned.1.call-start = ((), (), s32[]{:S(2)}) async-start(), calls=%async_computation.2 | async-start | bytes 983040 | tf_op jit(solution)/shard_map/reduce_scatter | solution.py:134
  86.8 2.7 %copy-start.3 = (bf16[2,128,1536]{2,1,0:T(8,128)(2,1)S(1)}, bf16[2,128,1536]{2,1,0:T(8,128)(2,1)}, u32[]{:S(2)}) copy-start(bf16[2,128,1536]{2,1,0:T(8,128)(2,1)} %all-reduce.2.cloned.1.call-done) | copy-start | bytes 2359300
  86.8 3.1 %copy-start.8 = (bf16[2,1536,384]{2,1,0:T(8,128)(2,1)S(1)}, bf16[2,1536,384]{2,1,0:T(8,128)(2,1)}, u32[]{:S(2)}) copy-start(bf16[2,1536,384]{2,1,0:T(8,128)(2,1)} %param.18) | copy-start | bytes 7077892
  89.4 0.7 copy-start.11
  90.1 10.3 %copy-start.9 = (bf16[384,1536]{1,0:T(8,128)(2,1)S(1)}, bf16[384,1536]{1,0:T(8,128)(2,1)}, u32[]{:S(2)}) copy-start(bf16[384,1536]{1,0:T(8,128)(2,1)} %param.22) | copy-start | bytes 3538948
  90.1 10.3 %copy-start.12 = (f32[384]{0:T(512)S(1)}, f32[384]{0:T(512)}, u32[]{:S(2)}) copy-start(f32[384]{0:T(512)} %param.21) | copy-start | bytes 4612
  90.1 10.3 %copy-start.13 = (f32[384]{0:T(512)S(1)}, f32[384]{0:T(512)}, u32[]{:S(2)}) copy-start(f32[384]{0:T(512)} %param.20) | copy-start | bytes 4612
  91.2 4.9 %collective-permute-start.3 = (bf16[2,15,384]{2,1,0:T(8,128)(2,1)S(1)}, bf16[2,15,384]{2,1,0:T(8,128)(2,1)S(1)}, u32[]{:S(2)}, u32[]{:S(2)}) collective-permute-start(bf16[2,15,384]{2,1,0:T(8,128)(2,1)S(1)} %get-tuple-element.41), channel_id=1, source_target_pairs={{0,4},{4,8},{8,12},{1,5},{5,9},{9,13},{2,6},{6,10},{10,14},{3,7},{... | collective-permute-start | bytes 69128 | tf_op jit(solution)/shard_map/ppermute | solution.py:45
  94.6 5.7 %collective-permute-start.4 = (bf16[2,15,384]{2,1,0:T(8,128)(2,1)S(1)}, bf16[2,15,384]{2,1,0:T(8,128)(2,1)S(1)}, u32[]{:S(2)}, u32[]{:S(2)}) collective-permute-start(bf16[2,15,384]{2,1,0:T(8,128)(2,1)S(1)} %get-tuple-element.42), channel_id=1, source_target_pairs={{4,0},{8,4},{12,8},{5,1},{9,5},{13,9},{6,2},{10,6},{14,10},{7,3},{... | collective-permute-start | bytes 69128 | tf_op jit(solution)/shard_map/ppermute | solution.py:46
  100.4 3.7 %copy-start.6 = (s32[1536]{0:T(1024)S(1)}, s32[1536]{0:T(1024)}, u32[]{:S(2)}) copy-start(s32[1536]{0:T(1024)} %param.23) | copy-start | bytes 18436
Sparse Core Ops, SparseCore 0:
  53.6 33.1 all-reduce.1
  104.0 22.3 reduce-scatter.1
